TPU v7x, 256 devices: a whole 4x4x8 slice. The times are simulated.
256 devices in a mesh: req: 8 (over z), exp: 8 (over y, core), hid: 4 (over x).
Axes of the slice: x: 4, y: 4, z: 8, core: 2. Of those that a mesh axis runs over, the one named last changes fastest.
Arguments:
- layer_input_rows: bfloat16 [16384, 1536], P(('req', 'exp')), may hold values from -6 to 6
- attention_norm_gain: float32 [1536], replicated
- query_weight: bfloat16 [1536, 1536], P(None, 'hid'), may hold values from -1 to 1
- key_weight: bfloat16 [1536, 512], P(None, 'hid'), may hold values from -1 to 1
- value_weight: bfloat16 [1536, 512], P(None, 'hid'), may hold values from -0.15625 to 0.15625
- attention_output_weight: bfloat16 [1536, 1536], P('hid'), may hold values from -0.15625 to 0.15625
- query_down_factor: bfloat16 [64, 1536, 16], P(('req', 'exp')), may hold values from -0.15625 to 0.15625
- query_up_factor: bfloat16 [64, 16, 1536], P(('req', 'exp')), may hold values from -1.5 to 1.5
- value_down_factor: bfloat16 [64, 1536, 16], P(('req', 'exp')), may hold values from -0.15625 to 0.15625
- value_up_factor: bfloat16 [64, 16, 512], P(('req', 'exp')), may hold values from -1.5 to 1.5
- lengths: int32 [8, 4], P('req'), may hold values from 1 to 1024, 2048 in all within a row
- request_adapter: int32 [8, 4], replicated, may hold values from 0 to 63
- adapter_home_row: int32 [64], replicated, may hold values from 0 to 63, each once
- expert_norm_gain: float32 [1536], replicated, may hold values from 0.4 to 1.6
- routes: int32 [16384, 8], P(('req', 'exp', 'hid')), may hold values from 0 to 39, all different within a row; in each aligned block of 64 rows (0 to 63, 64 to 127, ...) at most 16 rows name the same one
- router_expert_weight: float32 [16384, 8], P(('req', 'exp', 'hid')), may hold values from 0.1 to 0.5
- expert_gate_weight: bfloat16 [40, 1536, 512], P('exp', None, 'hid'), may hold values from -0.15625 to 0.15625
- expert_up_weight: bfloat16 [40, 1536, 512], P('exp', None, 'hid'), may hold values from -0.15625 to 0.15625
- expert_down_weight: bfloat16 [40, 512, 1536], P('exp', 'hid'), may hold values from -0.25 to 0.25
Outputs:
- attn_out: bfloat16 [16384, 1536], P(('req', 'exp', 'hid'))
- expert_out: bfloat16 [16384, 1536], P(('req', 'exp', 'hid'))
Inputs may be any that keep to these rules, and one draw needn't show every extreme that they name: `lengths`: each row sums to 2048; its largest entry is exactly 1024. `adapter_home_row`: each adapter row appears once. `routes`: A row names 8 different experts. In the rows of one device (64 consecutive rows, aligned) no expert is named more than 16 times, a bound that some block reaches in some of them.
All inputs are finite; a program needn't handle non-finite values.
Results may differ from a plain program's by a relative error of at most 0.029.
The roundings to bfloat16 on the way count: a program that leaves them out, or rounds other values in their place, can miss the bound.
Values may be sent and summed in bfloat16 or wider, within the bound.
No kernel may reach another device: no remote copies, remote signals or barrier semaphores. Data moves between devices by JAX's collectives and lax.ppermute only.
A program may use at most 128 MiB of HBM per device.

v0:
```python
import jax
import jax.numpy as jnp
from jax import lax
from jax.sharding import PartitionSpec as P

HEAD_WIDTH = 64
scale_attn = 0.015625
residual_mult = 0.22
norm_eps = 1e-06
rope_base = 10000.0
neg_large = -1e30


def rms_norm(values, norm_gain):
    widened = values.astype(jnp.float32)
    mean_sq = jnp.mean(widened * widened, axis=-1, keepdims=True)
    return (widened * lax.rsqrt(mean_sq + norm_eps) * norm_gain).astype(jnp.bfloat16)


def rotary(heads_in, position):
    half_size = heads_in.shape[-1] // 2
    frequency = rope_base ** (-2.0 * jnp.arange(half_size, dtype=jnp.float32) / heads_in.shape[-1])
    angles = position.astype(jnp.float32)[:, None] * frequency[None, :]
    cosine = jnp.cos(angles)[:, None, :]
    sine_part = jnp.sin(angles)[:, None, :]
    first_half = heads_in[..., :half_size]
    second_half = heads_in[..., half_size:]
    return jnp.concatenate(
        [
            first_half * cosine - second_half * sine_part,
            second_half * cosine + first_half * sine_part,
        ],
        axis=-1,
    )


def request_of(row_ids, group_len):
    request_end = jnp.cumsum(group_len)
    return jnp.sum((row_ids[:, None] >= request_end[None, :]).astype(jnp.int32), axis=1)


def locate(row_ids, group_len):
    request_end = jnp.cumsum(group_len)
    request_start = request_end - group_len
    request = request_of(row_ids, group_len)
    member = request[:, None] == jnp.arange(group_len.shape[0], dtype=jnp.int32)[None, :]
    position = row_ids - jnp.sum(jnp.where(member, request_start[None, :], 0), axis=1)
    return (request, member, position)


def expert_rows(rows_in, expert_gate_weight, expert_up_weight, expert_down_weight):
    gate_act = jnp.einsum(
        "red,edf->ref", rows_in, expert_gate_weight, preferred_element_type=jnp.float32
    )
    upper = jnp.einsum(
        "red,edf->ref", rows_in, expert_up_weight, preferred_element_type=jnp.float32
    )
    hidden = (jax.nn.silu(gate_act) * upper).astype(jnp.bfloat16)
    return jnp.einsum(
        "ref,efd->red", hidden, expert_down_weight, preferred_element_type=jnp.float32
    )


def per_device(
    layer_input_rows,
    attention_norm_gain,
    query_weight,
    key_weight,
    value_weight,
    attention_output_weight,
    query_down_factor,
    query_up_factor,
    value_down_factor,
    value_up_factor,
    lengths,
    request_adapter,
    adapter_home_row,
    expert_norm_gain,
    routes,
    router_expert_weight,
    expert_gate_weight,
    expert_up_weight,
    expert_down_weight,
):
    exp_count = lax.axis_size("exp")
    hid_count = lax.axis_size("hid")
    exp_index = lax.axis_index("exp")
    hid_index = lax.axis_index("hid")
    req_index = lax.axis_index("req")
    query_rows = layer_input_rows.shape[0]
    width = layer_input_rows.shape[1]
    kv_local = key_weight.shape[1] // HEAD_WIDTH
    q_local = query_weight.shape[1] // HEAD_WIDTH
    group_share = q_local // kv_local
    adapter_rank_size = query_down_factor.shape[2]
    requests = lengths.shape[1]
    group_len = lengths[0]
    row_ids = exp_index * query_rows + jnp.arange(query_rows, dtype=jnp.int32)
    request, member, position = locate(row_ids, group_len)
    wanted = lax.dynamic_index_in_dim(request_adapter, req_index, 0, keepdims=False)
    slot_ids = jnp.arange(adapter_home_row.shape[0], dtype=jnp.int32)
    home_of = jnp.sum(
        jnp.where(wanted[:, None] == slot_ids[None, :], adapter_home_row[None, :], 0), axis=1
    )
    query_cols = q_local * HEAD_WIDTH
    kv_cols = kv_local * HEAD_WIDTH
    bank_local = query_down_factor.shape[0]
    up_q = lax.dynamic_slice_in_dim(query_up_factor, hid_index * query_cols, query_cols, 2)
    up_v = lax.dynamic_slice_in_dim(value_up_factor, hid_index * kv_cols, kv_cols, 2)
    parts_in = (query_down_factor, up_q, value_down_factor, up_v)
    part_shapes = [p.shape[1:] for p in parts_in]
    part_sizes = [p.shape[1] * p.shape[2] for p in parts_in]
    bank = jnp.concatenate([p.reshape(bank_local, -1) for p in parts_in], axis=1)
    along_req = lax.all_gather(bank, "req", axis=0, tiled=True)
    home_dev = home_of // bank_local
    home_pick = home_dev // exp_count * bank_local + home_of % bank_local
    mine = home_dev % exp_count == exp_index
    rows_pick = jnp.take(along_req, home_pick, axis=0)
    rows_pick = jnp.where(mine[:, None], rows_pick, jnp.zeros_like(rows_pick))
    rows_all = lax.all_to_all(
        jnp.broadcast_to(rows_pick[None], (exp_count,) + rows_pick.shape),
        "exp",
        split_axis=0,
        concat_axis=0,
        tiled=True,
    )
    rows_pick = rows_all[home_dev % exp_count, jnp.arange(requests, dtype=jnp.int32)]
    chosen = []
    start = 0
    for shape_in, size_in in zip(part_shapes, part_sizes):
        chosen.append(rows_pick[:, start : start + size_in].reshape((requests,) + shape_in))
        start += size_in
    qa_sel, qb_sel, va_sel, vb_sel = chosen
    normed_rows = rms_norm(layer_input_rows, attention_norm_gain)

    def low_rank_term(a_sel, b_sel, width_cols, offset):
        inner_terms = jnp.einsum(
            "td,jdr->tjr", normed_rows, a_sel, preferred_element_type=jnp.float32
        )
        inner_terms = (
            jnp.where(member[:, :, None], inner_terms, 0.0)
            .reshape(query_rows, requests * adapter_rank_size)
            .astype(jnp.bfloat16)
        )
        right_factor = b_sel.reshape(requests * adapter_rank_size, width_cols)
        return jnp.dot(inner_terms, right_factor, preferred_element_type=jnp.float32)

    query_matrix = jnp.dot(
        normed_rows, query_weight, preferred_element_type=jnp.float32
    ) + low_rank_term(qa_sel, qb_sel, query_cols, hid_index * query_cols)
    query_matrix = rotary(query_matrix.reshape(query_rows, q_local, HEAD_WIDTH), position).astype(
        jnp.bfloat16
    )
    query_matrix = query_matrix.reshape(query_rows, kv_local, group_share, HEAD_WIDTH)
    keys_own = jnp.dot(normed_rows, key_weight, preferred_element_type=jnp.float32)
    keys_own = (
        rotary(keys_own.reshape(query_rows, kv_local, HEAD_WIDTH), position)
        .astype(jnp.bfloat16)
        .reshape(query_rows, kv_cols)
    )
    values_own = jnp.dot(
        normed_rows, value_weight, preferred_element_type=jnp.float32
    ) + low_rank_term(va_sel, vb_sel, kv_cols, hid_index * kv_cols)
    values_own = values_own.astype(jnp.bfloat16)
    running_max = jnp.full((kv_local, group_share, query_rows), neg_large, jnp.float32)
    kv_own = jnp.concatenate([keys_own, values_own], axis=1)
    kv_piece = lax.all_to_all(
        jnp.broadcast_to(kv_own[None], (exp_count,) + kv_own.shape),
        "exp",
        split_axis=0,
        concat_axis=0,
        tiled=True,
    ).reshape(exp_count * query_rows, 2 * kv_cols)
    key_piece = kv_piece[:, :kv_cols]
    value_piece = kv_piece[:, kv_cols:]
    piece_len = key_piece.shape[0]
    key_ids = jnp.arange(piece_len, dtype=jnp.int32)
    key_request = request_of(key_ids, group_len)
    allowed = (request[:, None] == key_request[None, :]) & (key_ids[None, :] <= row_ids[:, None])
    key_heads = key_piece.reshape(piece_len, kv_local, HEAD_WIDTH)
    value_heads = value_piece.reshape(piece_len, kv_local, HEAD_WIDTH)
    scores = (
        jnp.einsum("qkgh,nkh->kgqn", query_matrix, key_heads, preferred_element_type=jnp.float32)
        * scale_attn
    )
    scores = jnp.where(allowed[None, None], scores, neg_large)
    new_max = jnp.maximum(running_max, jnp.max(scores, axis=-1))
    weights = jnp.where(allowed[None, None], jnp.exp(scores - new_max[..., None]), 0.0)
    running_sum = jnp.sum(weights, axis=-1)
    running_out = jnp.einsum(
        "kgqn,nkh->kgqh",
        weights.astype(jnp.bfloat16),
        value_heads,
        preferred_element_type=jnp.float32,
    )
    running_max, running_sum, running_out = (new_max, running_sum, running_out)
    attended = (running_out / running_sum[..., None]).astype(jnp.bfloat16)
    attended = jnp.transpose(attended, (2, 0, 1, 3)).reshape(query_rows, query_cols)
    tok_rows = query_rows // hid_count
    head_sums = jnp.dot(attended, attention_output_weight, preferred_element_type=jnp.float32)
    head_sums = head_sums.astype(jnp.bfloat16).reshape(hid_count, tok_rows, width)
    head_sums = lax.all_to_all(head_sums, "hid", split_axis=0, concat_axis=0, tiled=True)
    attn_out = jnp.sum(head_sums.astype(jnp.float32), axis=0).astype(jnp.bfloat16)
    own_rows = lax.dynamic_slice_in_dim(layer_input_rows, hid_index * tok_rows, tok_rows, 0)
    mixed_rows = own_rows.astype(jnp.float32) + residual_mult * attn_out.astype(jnp.float32)
    normed_moe = rms_norm(mixed_rows, expert_norm_gain)
    local_exp = expert_gate_weight.shape[0]
    expert_count = local_exp * exp_count
    top_count = routes.shape[1]
    capacity = max(2, tok_rows // 4)
    flat_route = routes.reshape(tok_rows * top_count)
    route_hits = (flat_route[:, None] == jnp.arange(expert_count, dtype=jnp.int32)[None, :]).astype(
        jnp.int32
    )
    earlier = jnp.cumsum(route_hits, axis=0) - route_hits
    slot_pos = jnp.sum(earlier * route_hits, axis=1)
    slots = slot_pos * expert_count + flat_route
    slot_table = jnp.arange(capacity * expert_count, dtype=jnp.int32)
    placed = jnp.any(
        slot_table[:, None, None] == slots.reshape(tok_rows, top_count)[None], axis=2
    ).astype(jnp.bfloat16)
    outgoing = jnp.dot(placed, normed_moe, preferred_element_type=jnp.float32).astype(jnp.bfloat16)
    outgoing = outgoing.reshape(capacity, expert_count, width)
    partners = exp_count * hid_count
    halves = 2 if capacity % 2 == 0 else 1
    cap_part = capacity // halves
    slot_hit = slots.reshape(tok_rows, top_count)[:, :, None] == slot_table[None, None, :]
    combine = jnp.sum(jnp.where(slot_hit, router_expert_weight[:, :, None], 0.0), axis=1)
    expert_acc = jnp.zeros((tok_rows, width), jnp.float32)
    for half in range(halves):
        part_out = outgoing[half * cap_part : (half + 1) * cap_part]
        copies = jnp.broadcast_to(
            part_out.reshape(cap_part, exp_count, 1, local_exp, width),
            (cap_part, exp_count, hid_count, local_exp, width),
        )
        copies = copies.reshape(cap_part, partners * local_exp, width)
        arrived = lax.all_to_all(copies, ("exp", "hid"), split_axis=1, concat_axis=0, tiled=True)
        partials = expert_rows(
            arrived, expert_gate_weight, expert_up_weight, expert_down_weight
        ).astype(jnp.bfloat16)
        partials = jnp.transpose(
            partials.reshape(partners, cap_part, local_exp, width), (1, 0, 2, 3)
        ).reshape(cap_part, partners * local_exp, width)
        returned = lax.all_to_all(partials, ("exp", "hid"), split_axis=1, concat_axis=1, tiled=True)
        returned = returned.reshape(cap_part, exp_count, hid_count, local_exp, width)
        results = jnp.sum(returned.astype(jnp.float32), axis=2).astype(jnp.bfloat16)
        results = results.reshape(cap_part * expert_count, width)
        part_cols = combine[
            :, half * cap_part * expert_count : (half + 1) * cap_part * expert_count
        ]
        expert_acc = expert_acc + jnp.dot(
            part_cols,
            results.astype(jnp.float32),
            precision=lax.Precision.HIGHEST,
            preferred_element_type=jnp.float32,
        )
    expert_out = expert_acc.astype(jnp.bfloat16)
    return (attn_out, expert_out)


def solution(mesh):
    in_specs = (
        P(("req", "exp"), None),
        P(),
        P(None, "hid"),
        P(None, "hid"),
        P(None, "hid"),
        P("hid", None),
        P(("req", "exp"), None, None),
        P(("req", "exp"), None, None),
        P(("req", "exp"), None, None),
        P(("req", "exp"), None, None),
        P("req", None),
        P(),
        P(),
        P(),
        P(("req", "exp", "hid"), None),
        P(("req", "exp", "hid"), None),
        P("exp", None, "hid"),
        P("exp", None, "hid"),
        P("exp", "hid", None),
    )
    out_specs = (P(("req", "exp", "hid"), None), P(("req", "exp", "hid"), None))
    return jax.shard_map(
        per_device, mesh=mesh, in_specs=in_specs, out_specs=out_specs, check_vma=False
    )
```

profile of v0, /device:TPU:3, one launch (start us, length us, event | category | flops | bytes accessed | tf_op | source)
XLA Modules:
  0.0 396.5 jit_solution(12851483804816842418)
XLA Ops:
  5.1 28.5 %all-gather = bf16[8,1,57344]{2,1,0:T(2,128)(2,1)S(1)} all-gather(bf16[1,1,57344]{2,1,0:T(2,128)(2,1)S(1)} %maximum_bitcast_fusion), channel_id=1, replica_groups=mesh['req'=8,'exp'=8,'hid'=4] {'req'}, dimensions={0}, use_global_device_ids=true | all-gather | bytes 1032192 | tf_op jit(solution)/shard_map/all_gather | solution.py:114
  36.4 2.8 broadcast_in_dim.172
  39.2 9.0 %all-to-all-start = ((bf16[8,4,57344]{2,1,0:T(4,128)(2,1)}), bf16[8,4,57344]{2,1,0:T(4,128)(2,1)}, u32[]{:S(2)}, u32[]{:S(2)}) async-start(bf16[8,4,57344]{2,1,0:T(4,128)(2,1)} %broadcast_in_dim.172), calls=%async_computation | async-start | bytes 7340032 | tf_op jit(solution)/shard_map/all_to_all | solution.py:120
  53.8 37.6 %all-to-all-done = bf16[8,4,57344]{2,1,0:T(4,128)(2,1)} async-done(((bf16[8,4,57344]{2,1,0:T(4,128)(2,1)}), bf16[8,4,57344]{2,1,0:T(4,128)(2,1)}, u32[]{:S(2)}, u32[]{:S(2)}) %all-to-all-start) | async-done | bytes 3670048 | tf_op jit(solution)/shard_map/all_to_all | solution.py:120
  91.4 3.0 gather_fusion.1
  98.6 2.2 fusion.106
  109.3 4.4 %all-to-all-start.1 = ((bf16[8,256,256]{1,2,0:T(8,128)(2,1)}), bf16[8,256,256]{1,2,0:T(8,128)(2,1)S(1)}, u32[]{:S(2)}, u32[]{:S(2)}) async-start(bf16[8,256,256]{1,2,0:T(8,128)(2,1)} %broadcast_in_dim.174), calls=%async_computation.1 | async-start | bytes 2097152 | tf_op jit(solution)/shard_map/all_to_all | solution.py:167
  122.8 5.9 %all-to-all-done.1 = bf16[8,256,256]{1,2,0:T(8,128)(2,1)S(1)} async-done(((bf16[8,256,256]{1,2,0:T(8,128)(2,1)}), bf16[8,256,256]{1,2,0:T(8,128)(2,1)S(1)}, u32[]{:S(2)}, u32[]{:S(2)}) %all-to-all-start.1) | async-done | bytes 1048608 | tf_op jit(solution)/shard_map/all_to_all | solution.py:167
  132.5 3.0 fusion
  135.5 3.1 fusion.1
  138.7 3.6 fusion.57
  143.8 4.4 %all-to-all-start.2 = ((bf16[4,64,1536]{2,1,0:T(8,128)(2,1)}), bf16[4,64,1536]{2,1,0:T(8,128)(2,1)S(1)}, u32[]{:S(2)}, u32[]{:S(2)}) async-start(bf16[4,64,1536]{2,1,0:T(8,128)(2,1)} %bitcast.32), calls=%async_computation.2 | async-start | bytes 1572864 | tf_op jit(solution)/shard_map/all_to_all | solution.py:202
  150.6 7.5 %all-to-all-done.2 = bf16[4,64,1536]{2,1,0:T(8,128)(2,1)S(1)} async-done(((bf16[4,64,1536]{2,1,0:T(8,128)(2,1)}), bf16[4,64,1536]{2,1,0:T(8,128)(2,1)S(1)}, u32[]{:S(2)}, u32[]{:S(2)}) %all-to-all-start.2) | async-done | bytes 786464 | tf_op jit(solution)/shard_map/all_to_all | solution.py:202
  164.7 2.2 broadcast_in_dim.181
  166.9 7.6 %all-to-all-start.3 = ((bf16[8,160,1536]{2,0,1:T(8,128)(2,1)}), bf16[8,160,1536]{2,0,1:T(8,128)(2,1)}, u32[]{:S(2)}, u32[]{:S(2)}) async-start(bf16[8,160,1536]{2,0,1:T(8,128)(2,1)} %bitcast.213), calls=%async_computation.3 | async-start | bytes 7864320 | tf_op jit(solution)/shard_map/all_to_all | solution.py:237
  177.7 44.9 %all-to-all-done.3 = bf16[8,160,1536]{2,0,1:T(8,128)(2,1)} async-done(((bf16[8,160,1536]{2,0,1:T(8,128)(2,1)}), bf16[8,160,1536]{2,0,1:T(8,128)(2,1)}, u32[]{:S(2)}, u32[]{:S(2)}) %all-to-all-start.3) | async-done | bytes 3932192 | tf_op jit(solution)/shard_map/all_to_all | solution.py:237
  222.7 3.5 broadcast_in_dim.183
  226.1 5.1 %all-to-all-start.5 = ((bf16[8,160,1536]{2,0,1:T(8,128)(2,1)}), bf16[8,160,1536]{2,0,1:T(8,128)(2,1)}, u32[]{:S(2)}, u32[]{:S(2)}) async-start(bf16[8,160,1536]{2,0,1:T(8,128)(2,1)} %bitcast.212), calls=%async_computation.5 | async-start | bytes 7864320 | tf_op jit(solution)/shard_map/all_to_all | solution.py:237
  231.2 3.9 fusion.26
  235.1 6.8 %fusion.14 = bf16[32,8,5,1536]{3,1,0,2:T(8,128)(2,1)} fusion(bf16[5,128,1536]{2,1,0:T(8,128)(2,1)S(1)} %copy-done, bf16[5,1536,128]{2,1,0:T(8,128)(2,1)} %param.36, bf16[32,8,5,1536]{3,1,2,0:T(8,128)(2,1)} %bitcast.36, f32[256,5,128]{2,0,1:T(8,128)S(1)} %fusion.26), kind=kOutput, calls=%fused_computation.19 | convolution fusion | flops 1009582080 | bytes 12451840 | tf_op jit(solution)/shard_map/ref,efd->red/dot_general | solution.py:59
  241.9 4.3 %copy.103 = bf16[32,8,5,1536]{3,1,2,0:T(8,128)(2,1)} copy(bf16[32,8,5,1536]{3,1,0,2:T(8,128)(2,1)} %fusion.14) | data formatting | bytes 7864320 | tf_op jit(solution)/shard_map/reshape | solution.py:242
  246.3 32.8 %all-to-all-done.5 = bf16[8,160,1536]{2,0,1:T(8,128)(2,1)} async-done(((bf16[8,160,1536]{2,0,1:T(8,128)(2,1)}), bf16[8,160,1536]{2,0,1:T(8,128)(2,1)}, u32[]{:S(2)}, u32[]{:S(2)}) %all-to-all-start.5) | async-done | bytes 3932192 | tf_op jit(solution)/shard_map/all_to_all | solution.py:237
  279.1 5.1 %all-to-all-start.4 = ((bf16[8,160,1536]{2,0,1:T(8,128)(2,1)}), bf16[8,160,1536]{2,0,1:T(8,128)(2,1)}, u32[]{:S(2)}, u32[]{:S(2)}) async-start(bf16[8,160,1536]{2,0,1:T(8,128)(2,1)} %bitcast.211), calls=%async_computation.4 | async-start | bytes 7864320 | tf_op jit(solution)/shard_map/all_to_all | solution.py:244
  284.2 3.9 fusion.32
  288.1 6.9 %fusion.15 = bf16[32,8,5,1536]{3,1,0,2:T(8,128)(2,1)} fusion(bf16[5,128,1536]{2,1,0:T(8,128)(2,1)S(1)} %copy-done, bf16[5,1536,128]{2,1,0:T(8,128)(2,1)} %param.36, bf16[32,8,5,1536]{3,1,2,0:T(8,128)(2,1)} %bitcast.47, f32[256,5,128]{2,0,1:T(8,128)S(1)} %fusion.32), kind=kOutput, calls=%fused_computation.20 | convolution fusion | flops 1009582080 | bytes 12451840 | tf_op jit(solution)/shard_map/ref,efd->red/dot_general | solution.py:59
  295.0 4.3 %copy.107 = bf16[32,8,5,1536]{3,1,2,0:T(8,128)(2,1)} copy(bf16[32,8,5,1536]{3,1,0,2:T(8,128)(2,1)} %fusion.15) | data formatting | bytes 7864320 | tf_op jit(solution)/shard_map/reshape | solution.py:242
  299.3 32.9 %all-to-all-done.4 = bf16[8,160,1536]{2,0,1:T(8,128)(2,1)} async-done(((bf16[8,160,1536]{2,0,1:T(8,128)(2,1)}), bf16[8,160,1536]{2,0,1:T(8,128)(2,1)}, u32[]{:S(2)}, u32[]{:S(2)}) %all-to-all-start.4) | async-done | bytes 3932192 | tf_op jit(solution)/shard_map/all_to_all | solution.py:244
  332.2 5.2 %all-to-all-start.6 = ((bf16[8,160,1536]{2,0,1:T(8,128)(2,1)}), bf16[8,160,1536]{2,0,1:T(8,128)(2,1)}, u32[]{:S(2)}, u32[]{:S(2)}) async-start(bf16[8,160,1536]{2,0,1:T(8,128)(2,1)} %bitcast.210), calls=%async_computation.6 | async-start | bytes 7864320 | tf_op jit(solution)/shard_map/all_to_all | solution.py:244
  338.7 4.0 %reduce_sum.130 = bf16[8,8,5,1536]{3,0,2,1:T(8,128)(2,1)} reduce(bf16[8,8,4,5,1536]{4,0,3,2,1:T(8,128)(2,1)} %bitcast.44, bf16[]{:T(256)} %constant.140.clone.1), dimensions={2}, to_apply=%region_15.16 | reduce | flops 1474560 | bytes 4915202 | tf_op jit(solution)/shard_map/reduce_sum | solution.py:246
  345.4 40.0 %all-to-all-done.6 = bf16[8,160,1536]{2,0,1:T(8,128)(2,1)} async-done(((bf16[8,160,1536]{2,0,1:T(8,128)(2,1)}), bf16[8,160,1536]{2,0,1:T(8,128)(2,1)}, u32[]{:S(2)}, u32[]{:S(2)}) %all-to-all-start.6) | async-done | bytes 3932192 | tf_op jit(solution)/shard_map/all_to_all | solution.py:244
  385.4 4.0 %reduce_sum.131 = bf16[8,8,5,1536]{3,0,2,1:T(8,128)(2,1)} reduce(bf16[8,8,4,5,1536]{4,0,3,2,1:T(8,128)(2,1)} %bitcast.55, bf16[]{:T(256)} %constant.140.clone.1), dimensions={2}, to_apply=%region_16.17 | reduce | flops 1474560 | bytes 4915202 | tf_op jit(solution)/shard_map/reduce_sum | solution.py:246
  394.2 2.3 fusion.20
  (156 shorter events, 60.4 us)
Async XLA Ops:
  0.6 234.5 %copy-start = (bf16[5,128,1536]{2,1,0:T(8,128)(2,1)S(1)}, bf16[5,128,1536]{2,1,0:T(8,128)(2,1)}, u32[]{:S(2)}) copy-start(bf16[5,128,1536]{2,1,0:T(8,128)(2,1)} %param.37) | copy-start | bytes 5898244
  5.1 29.6 %copy-start.24 = (s32[8,4]{0,1:T(4,128)S(1)}, s32[8,4]{0,1:T(4,128)}, u32[]{:S(2)}) copy-start(s32[8,4]{0,1:T(4,128)} %param.30) | copy-start | bytes 388
  5.1 29.8 %copy-start.32 = (s32[64]{0:T(128)S(1)}, s32[64]{0:T(128)}, u32[]{:S(2)}) copy-start(s32[64]{0:T(128)} %param.31) | copy-start | bytes 772
  39.2 9.0 %copy-start.33 = (s32[1,4]{1,0:T(1,128)S(1)}, s32[1,4]{1,0:T(1,128)}, u32[]{:S(2)}) copy-start(s32[1,4]{1,0:T(1,128)} %param.29) | copy-start | bytes 52
  39.2 9.2 %copy-start.22 = (s32[64,8]{0,1:T(8,128)S(1)}, s32[64,8]{0,1:T(8,128)}, u32[]{:S(2)}) copy-start(s32[64,8]{0,1:T(8,128)} %param.33) | copy-start | bytes 6148
  39.2 10.9 %copy-start.4 = (bf16[256,1536]{1,0:T(8,128)(2,1)S(1)}, bf16[256,1536]{1,0:T(8,128)(2,1)}, u32[]{:S(2)}) copy-start(bf16[256,1536]{1,0:T(8,128)(2,1)} %param.19) | copy-start | bytes 2359300
  39.2 11.4 %copy-start.28 = (bf16[1536,128]{1,0:T(8,128)(2,1)S(1)}, bf16[1536,128]{1,0:T(8,128)(2,1)}, u32[]{:S(2)}) copy-start(bf16[1536,128]{1,0:T(8,128)(2,1)} %param.22) | copy-start | bytes 1179652
  39.2 11.4 %copy-start.30 = (f32[1536]{0:T(1024)S(1)}, f32[1536]{0:T(1024)}, u32[]{:S(2)}) copy-start(f32[1536]{0:T(1024)} %param.20) | copy-start | bytes 18436
  39.2 52.2 %all-to-all-start = ((bf16[8,4,57344]{2,1,0:T(4,128)(2,1)}), bf16[8,4,57344]{2,1,0:T(4,128)(2,1)}, u32[]{:S(2)}, u32[]{:S(2)}) async-start(bf16[8,4,57344]{2,1,0:T(4,128)(2,1)} %broadcast_in_dim.172), calls=%async_computation | async-start | bytes 7340032 | tf_op jit(solution)/shard_map/all_to_all | solution.py:120
  48.5 5.3 %copy-start.7 = (s32[64,8]{1,0:T(8,128)}, s32[64,8]{1,0:T(8,128)S(1)}, u32[]{:S(2)}) copy-start(s32[64,8]{1,0:T(8,128)S(1)} %copy.96) | copy-start | bytes 6148
  49.2 4.6 %copy-start.20 = (s32[256]{0:T(256)}, s32[256]{0:T(256)S(1)}, u32[]{:S(2)}) copy-start(s32[256]{0:T(256)S(1)} %iota_add_fusion) | copy-start | bytes 3076
  50.3 48.3 %copy-start.25 = (f32[256]{0:T(256)}, f32[256]{0:T(256)S(1)}, u32[]{:S(2)}) copy-start(f32[256]{0:T(256)S(1)} %add_rsqrt_fusion) | copy-start | bytes 3076
  104.2 3.4 copy-start.26
  104.2 3.5 copy-start.29
  104.2 3.5 copy-start.31
  104.2 4.0 %copy-start.14 = (bf16[256,2,64]{0,2,1:T(8,128)(2,1)S(1)}, bf16[256,2,64]{0,2,1:T(8,128)(2,1)}, u32[]{:S(2)}) copy-start(bf16[256,2,64]{0,2,1:T(8,128)(2,1)} %pad_maximum_fusion.1) | copy-start | bytes 196612
  108.2 5.5 %copy-start.15 = (s32[2048]{0:T(1024)S(1)}, s32[2048]{0:T(1024)}, u32[]{:S(2)}) copy-start(s32[2048]{0:T(1024)} %convert_reduce_fusion) | copy-start | bytes 24580
  108.2 5.5 %copy-start.17 = (s32[256]{0:T(256)S(1)}, s32[256]{0:T(256)}, u32[]{:S(2)}) copy-start(s32[256]{0:T(256)} %copy-done.16) | copy-start | bytes 3076
  108.2 5.5 %copy-start.21 = (s32[256]{0:T(256)S(1)}, s32[256]{0:T(256)}, u32[]{:S(2)}) copy-start(s32[256]{0:T(256)} %copy-done.20) | copy-start | bytes 3076
  109.3 19.4 %all-to-all-start.1 = ((bf16[8,256,256]{1,2,0:T(8,128)(2,1)}), bf16[8,256,256]{1,2,0:T(8,128)(2,1)S(1)}, u32[]{:S(2)}, u32[]{:S(2)}) async-start(bf16[8,256,256]{1,2,0:T(8,128)(2,1)} %broadcast_in_dim.174), calls=%async_computation.1 | async-start | bytes 2097152 | tf_op jit(solution)/shard_map/all_to_all | solution.py:167
  138.7 3.7 copy-start.6
  142.3 5.9 %copy-start.19 = (s32[4,128]{1,0:T(4,128)S(1)}, s32[4,128]{1,0:T(4,128)}, u32[]{:S(2)}) copy-start(s32[4,128]{1,0:T(4,128)} %eq.130) | copy-start | bytes 6148
  142.3 5.9 %copy-start.8 = (s32[64,8]{1,0:T(8,128)S(1)}, s32[64,8]{1,0:T(8,128)}, u32[]{:S(2)}) copy-start(s32[64,8]{1,0:T(8,128)} %copy-done.7) | copy-start | bytes 6148
  143.8 15.7 %copy-start.18 = (f32[1536]{0:T(1024)S(1)}, f32[1536]{0:T(1024)}, u32[]{:S(2)}) copy-start(f32[1536]{0:T(1024)} %param.32) | copy-start | bytes 18436
  143.8 14.4 %all-to-all-start.2 = ((bf16[4,64,1536]{2,1,0:T(8,128)(2,1)}), bf16[4,64,1536]{2,1,0:T(8,128)(2,1)S(1)}, u32[]{:S(2)}, u32[]{:S(2)}) async-start(bf16[4,64,1536]{2,1,0:T(8,128)(2,1)} %bitcast.32), calls=%async_computation.2 | async-start | bytes 1572864 | tf_op jit(solution)/shard_map/all_to_all | solution.py:202
  158.3 4.3 %copy-start.3 = (bf16[64,1536]{1,0:T(8,128)(2,1)}, bf16[64,1536]{1,0:T(8,128)(2,1)S(1)}, u32[]{:S(2)}) copy-start(bf16[64,1536]{1,0:T(8,128)(2,1)S(1)} %reduce_sum.126) | copy-start | bytes 589828
  166.9 55.7 %all-to-all-start.3 = ((bf16[8,160,1536]{2,0,1:T(8,128)(2,1)}), bf16[8,160,1536]{2,0,1:T(8,128)(2,1)}, u32[]{:S(2)}, u32[]{:S(2)}) async-start(bf16[8,160,1536]{2,0,1:T(8,128)(2,1)} %bitcast.213), calls=%async_computation.3 | async-start | bytes 7864320 | tf_op jit(solution)/shard_map/all_to_all | solution.py:237
  226.1 53.0 %all-to-all-start.5 = ((bf16[8,160,1536]{2,0,1:T(8,128)(2,1)}), bf16[8,160,1536]{2,0,1:T(8,128)(2,1)}, u32[]{:S(2)}, u32[]{:S(2)}) async-start(bf16[8,160,1536]{2,0,1:T(8,128)(2,1)} %bitcast.212), calls=%async_computation.5 | async-start | bytes 7864320 | tf_op jit(solution)/shard_map/all_to_all | solution.py:237
  279.1 53.1 %all-to-all-start.4 = ((bf16[8,160,1536]{2,0,1:T(8,128)(2,1)}), bf16[8,160,1536]{2,0,1:T(8,128)(2,1)}, u32[]{:S(2)}, u32[]{:S(2)}) async-start(bf16[8,160,1536]{2,0,1:T(8,128)(2,1)} %bitcast.211), calls=%async_computation.4 | async-start | bytes 7864320 | tf_op jit(solution)/shard_map/all_to_all | solution.py:244
  332.2 5.3 %copy-start.23 = (f32[64,8]{0,1:T(8,128)S(1)}, f32[64,8]{0,1:T(8,128)}, u32[]{:S(2)}) copy-start(f32[64,8]{0,1:T(8,128)} %param.34) | copy-start | bytes 6148
  332.2 5.4 %copy-start.11 = (s32[64,8]{1,0:T(8,128)S(1)}, s32[64,8]{1,0:T(8,128)}, u32[]{:S(2)}) copy-start(s32[64,8]{1,0:T(8,128)} %copy-done.10) | copy-start | bytes 6148
  332.2 53.2 %all-to-all-start.6 = ((bf16[8,160,1536]{2,0,1:T(8,128)(2,1)}), bf16[8,160,1536]{2,0,1:T(8,128)(2,1)}, u32[]{:S(2)}, u32[]{:S(2)}) async-start(bf16[8,160,1536]{2,0,1:T(8,128)(2,1)} %bitcast.210), calls=%async_computation.6 | async-start | bytes 7864320 | tf_op jit(solution)/shard_map/all_to_all | solution.py:244
  (10 other events, 19.4 us)
where the time goes:
time: 398 us; the launch traced here: 397 us
  waiting for transfers between devices  202 us (51%)
  local copies, waits for them, and re-layouts  57.4 us (14%)
  matrix products  44.1 us (11%)
  starting transfers between devices  40.9 us (10%)
  blocking collectives  28.5 us (7%)
  other arithmetic  22.6 us (6%)
    all_to_all x2, waiting for transfers between devices, per_device(): lax.all_to_all(copies, ('exp', 'hid'), split_axis=1, concat_axis=0, tiled...  77.8 us
    all_to_all x2, waiting for transfers between devices, per_device(): lax.all_to_all(partials, ('exp', 'hid'), split_axis=1, concat_axis=1, til...  72.8 us
    all_to_all x1, waiting for transfers between devices, per_device(): lax.all_to_all(jnp.broadcast_to(rows_pick[None], (exp_count,) + rows_pick...  37.6 us
    all_gather x1, blocking collectives, per_device(): along_req = lax.all_gather(bank, 'req', axis=0, tiled=True)  28.5 us
    dot_general x2, matrix products, expert_rows(): jnp.einsum('ref,efd->red', hidden, expert_down_weight, preferred_element_...  13.7 us
    all_to_all x2, starting transfers between devices, per_device(): lax.all_to_all(copies, ('exp', 'hid'), split_axis=1, concat_axis=0, tiled...  12.7 us
    broadcast_in_dim x6, local copies, waits for them, and re-layouts, per_device(): jnp.broadcast_to(part_out.reshape(cap_part, exp_count, 1, local_exp, widt...  10.9 us
    all_to_all x2, starting transfers between devices, per_device(): lax.all_to_all(partials, ('exp', 'hid'), split_axis=1, concat_axis=1, til...  10.4 us
  transfers between devices with their start and end apart: 7, of which 7 were waited for; matrix products, arithmetic and copies ran while one was open for 15% of the time, Pallas kernels for 0%

commit v1 on v0

--- a/solution.py
+++ b/solution.py
@@ -9,6 +9,15 @@
 norm_eps = 1e-06
 rope_base = 10000.0
 neg_large = -1e30
+extend_table = lambda piece_in, comm_axis, d_out: jnp.concatenate(
+    jax.lax.all_to_all(
+        jnp.stack([piece_in for _ in range(jax.lax.axis_size(comm_axis))]),
+        concat_axis=0,
+        axis_name=comm_axis,
+        split_axis=0,
+    ),
+    d_out,
+)
 
 
 def rms_norm(values, norm_gain):
@@ -111,7 +120,7 @@
     part_shapes = [p.shape[1:] for p in parts_in]
     part_sizes = [p.shape[1] * p.shape[2] for p in parts_in]
     bank = jnp.concatenate([p.reshape(bank_local, -1) for p in parts_in], axis=1)
-    along_req = lax.all_gather(bank, "req", axis=0, tiled=True)
+    along_req = extend_table(bank, "req", 0)
     home_dev = home_of // bank_local
     home_pick = home_dev // exp_count * bank_local + home_of % bank_local
     mine = home_dev % exp_count == exp_index

time: 398 us -> 425 us (1.068); the launches traced: 397 us -> 417 us
  blocking collectives: 28.5 us -> 0 us
  waiting for transfers between devices: 202 us -> 227 us
  local copies, waits for them, and re-layouts: 57.4 us -> 66.6 us
  other arithmetic: 22.6 us -> 30.6 us
  starting transfers between devices: 40.9 us -> 46.7 us
    all_gather x1 -> x0, blocking collectives: 28.5 us -> none  [per_device(): along_req = lax.all_gather(bank, 'req', axis=0, tiled=True)]
    all_to_all x0 -> x1, waiting for transfers between devices: none -> 25.9 us  [jax.lax.all_to_all(jnp.stack([piece_in for _ in range(jax.lax.axis_size(c...]
    all_to_all x0 -> x1, starting transfers between devices: none -> 8.74 us  [jax.lax.all_to_all(jnp.stack([piece_in for _ in range(jax.lax.axis_size(c...]
    another operation x5 -> x6, other arithmetic: 3.16 us -> 10.7 us  [the longest x1 7.52 us: jnp.stack([piece_in for _ in range(jax.lax.axis_size(comm_axis))])]
    unnamed x77 -> x79, local copies, waits for them, and re-layouts: 5.17 us -> 11.6 us
  transfers between devices with their start and end apart: 7 -> 8, of which waited for: 7 -> 8; matrix products, arithmetic and copies ran while one was open for 15% -> 14% of each run, Pallas kernels for 0% -> 0%
where the time goes in v1:
time: 425 us; the launch traced here: 417 us
  waiting for transfers between devices  227 us (53%)
  local copies, waits for them, and re-layouts  66.6 us (16%)
  starting transfers between devices  46.7 us (11%)
  matrix products  44.1 us (10%)
  other arithmetic  30.6 us (7%)
    all_to_all x2, waiting for transfers between devices, per_device(): lax.all_to_all(copies, ('exp', 'hid'), split_axis=1, concat_axis=0, tiled...  77.6 us
    all_to_all x2, waiting for transfers between devices, per_device(): lax.all_to_all(partials, ('exp', 'hid'), split_axis=1, concat_axis=1, til...  72.6 us
    all_to_all x1, waiting for transfers between devices, per_device(): lax.all_to_all(jnp.broadcast_to(rows_pick[None], (exp_count,) + rows_pick...  37.6 us
    all_to_all x1, waiting for transfers between devices, jax.lax.all_to_all(jnp.stack([piece_in for _ in range(jax.lax.axis_size(c...  25.9 us
    dot_general x2, matrix products, expert_rows(): jnp.einsum('ref,efd->red', hidden, expert_down_weight, preferred_element_...  13.7 us
    all_to_all x2, starting transfers between devices, per_device(): lax.all_to_all(copies, ('exp', 'hid'), split_axis=1, concat_axis=0, tiled...  13 us
    unnamed x79, local copies, waits for them, and re-layouts  11.6 us
    broadcast_in_dim x6, local copies, waits for them, and re-layouts, per_device(): jnp.broadcast_to(part_out.reshape(cap_part, exp_count, 1, local_exp, widt...  10.9 us
  transfers between devices with their start and end apart: 8, of which 8 were waited for; matrix products, arithmetic and copies ran while one was open for 14% of the time, Pallas kernels for 0%

profile of v1, /device:TPU:3, one launch (start us, length us, event | category | flops | bytes accessed | tf_op | source)
XLA Modules:
  0.0 416.7 jit_solution(8997145442299503796)
XLA Ops:
  8.2 7.5 %reduce.9 = bf16[8,57344]{1,0:T(8,128)(2,1)S(1)} reduce(bf16[8,1,57344]{2,1,0:T(2,128)(2,1)} %stack.2, bf16[]{:T(256)} %broadcast.484), dimensions={1}, to_apply=%stack.2.reduce_sub_computation | reduce | bytes 1835010 | tf_op jit(solution)/shard_map/stack | solution.py:14
  17.5 8.7 %all-to-all-start = ((bf16[8,2,28672]{2,1,0:T(2,128)(2,1)}), bf16[8,2,28672]{2,1,0:T(2,128)(2,1)S(1)}, u32[]{:S(2)}, u32[]{:S(2)}) async-start(bf16[8,2,28672]{2,1,0:T(2,128)(2,1)} %reshape.472), calls=%async_computation | async-start | bytes 1835008 | tf_op jit(solution)/shard_map/all_to_all | solution.py:13
  26.6 25.9 %all-to-all-done = bf16[8,2,28672]{2,1,0:T(2,128)(2,1)S(1)} async-done(((bf16[8,2,28672]{2,1,0:T(2,128)(2,1)}), bf16[8,2,28672]{2,1,0:T(2,128)(2,1)S(1)}, u32[]{:S(2)}, u32[]{:S(2)}) %all-to-all-start) | async-done | bytes 917536 | tf_op jit(solution)/shard_map/all_to_all | solution.py:13
  52.5 3.3 reshape.473
  59.6 2.8 broadcast_in_dim.172
  62.5 5.1 %all-to-all-start.1 = ((bf16[8,4,57344]{2,1,0:T(4,128)(2,1)}), bf16[8,4,57344]{2,1,0:T(4,128)(2,1)}, u32[]{:S(2)}, u32[]{:S(2)}) async-start(bf16[8,4,57344]{2,1,0:T(4,128)(2,1)} %broadcast_in_dim.172), calls=%async_computation.1 | async-start | bytes 7340032 | tf_op jit(solution)/shard_map/all_to_all | solution.py:129
  73.1 37.6 %all-to-all-done.1 = bf16[8,4,57344]{2,1,0:T(4,128)(2,1)} async-done(((bf16[8,4,57344]{2,1,0:T(4,128)(2,1)}), bf16[8,4,57344]{2,1,0:T(4,128)(2,1)}, u32[]{:S(2)}, u32[]{:S(2)}) %all-to-all-start.1) | async-done | bytes 3670048 | tf_op jit(solution)/shard_map/all_to_all | solution.py:129
  110.7 2.9 gather_fusion.1
  128.6 4.6 %all-to-all-start.2 = ((bf16[8,256,256]{1,2,0:T(8,128)(2,1)}), bf16[8,256,256]{1,2,0:T(8,128)(2,1)S(1)}, u32[]{:S(2)}, u32[]{:S(2)}) async-start(bf16[8,256,256]{1,2,0:T(8,128)(2,1)} %broadcast_in_dim.174), calls=%async_computation.2 | async-start | bytes 2097152 | tf_op jit(solution)/shard_map/all_to_all | solution.py:176
  142.4 5.8 %all-to-all-done.2 = bf16[8,256,256]{1,2,0:T(8,128)(2,1)S(1)} async-done(((bf16[8,256,256]{1,2,0:T(8,128)(2,1)}), bf16[8,256,256]{1,2,0:T(8,128)(2,1)S(1)}, u32[]{:S(2)}, u32[]{:S(2)}) %all-to-all-start.2) | async-done | bytes 1048608 | tf_op jit(solution)/shard_map/all_to_all | solution.py:176
  152.0 3.0 fusion
  155.0 3.1 fusion.1
  158.2 3.6 fusion.57
  163.3 4.4 %all-to-all-start.3 = ((bf16[4,64,1536]{2,1,0:T(8,128)(2,1)}), bf16[4,64,1536]{2,1,0:T(8,128)(2,1)S(1)}, u32[]{:S(2)}, u32[]{:S(2)}) async-start(bf16[4,64,1536]{2,1,0:T(8,128)(2,1)} %bitcast.31), calls=%async_computation.3 | async-start | bytes 1572864 | tf_op jit(solution)/shard_map/all_to_all | solution.py:211
  170.1 7.5 %all-to-all-done.3 = bf16[4,64,1536]{2,1,0:T(8,128)(2,1)S(1)} async-done(((bf16[4,64,1536]{2,1,0:T(8,128)(2,1)}), bf16[4,64,1536]{2,1,0:T(8,128)(2,1)S(1)}, u32[]{:S(2)}, u32[]{:S(2)}) %all-to-all-start.3) | async-done | bytes 786464 | tf_op jit(solution)/shard_map/all_to_all | solution.py:211
  186.4 7.6 %all-to-all-start.4 = ((bf16[8,160,1536]{2,0,1:T(8,128)(2,1)}), bf16[8,160,1536]{2,0,1:T(8,128)(2,1)}, u32[]{:S(2)}, u32[]{:S(2)}) async-start(bf16[8,160,1536]{2,0,1:T(8,128)(2,1)} %bitcast.211), calls=%async_computation.4 | async-start | bytes 7864320 | tf_op jit(solution)/shard_map/all_to_all | solution.py:246
  197.2 44.9 %all-to-all-done.4 = bf16[8,160,1536]{2,0,1:T(8,128)(2,1)} async-done(((bf16[8,160,1536]{2,0,1:T(8,128)(2,1)}), bf16[8,160,1536]{2,0,1:T(8,128)(2,1)}, u32[]{:S(2)}, u32[]{:S(2)}) %all-to-all-start.4) | async-done | bytes 3932192 | tf_op jit(solution)/shard_map/all_to_all | solution.py:246
  242.1 3.5 broadcast_in_dim.183
  245.6 5.4 %all-to-all-start.6 = ((bf16[8,160,1536]{2,0,1:T(8,128)(2,1)}), bf16[8,160,1536]{2,0,1:T(8,128)(2,1)}, u32[]{:S(2)}, u32[]{:S(2)}) async-start(bf16[8,160,1536]{2,0,1:T(8,128)(2,1)} %bitcast.210), calls=%async_computation.6 | async-start | bytes 7864320 | tf_op jit(solution)/shard_map/all_to_all | solution.py:246
  251.1 3.9 fusion.26
  255.0 6.8 %fusion.14 = bf16[32,8,5,1536]{3,1,0,2:T(8,128)(2,1)} fusion(bf16[5,128,1536]{2,1,0:T(8,128)(2,1)S(1)} %copy-done, bf16[5,1536,128]{2,1,0:T(8,128)(2,1)} %param.36, bf16[32,8,5,1536]{3,1,2,0:T(8,128)(2,1)} %bitcast.35, f32[256,5,128]{2,0,1:T(8,128)S(1)} %fusion.26), kind=kOutput, calls=%fused_computation.19 | convolution fusion | flops 1009582080 | bytes 12451840 | tf_op jit(solution)/shard_map/ref,efd->red/dot_general | solution.py:68
  261.8 4.3 %copy.103 = bf16[32,8,5,1536]{3,1,2,0:T(8,128)(2,1)} copy(bf16[32,8,5,1536]{3,1,0,2:T(8,128)(2,1)} %fusion.14) | data formatting | bytes 7864320 | tf_op jit(solution)/shard_map/reshape | solution.py:251
  266.2 32.6 %all-to-all-done.6 = bf16[8,160,1536]{2,0,1:T(8,128)(2,1)} async-done(((bf16[8,160,1536]{2,0,1:T(8,128)(2,1)}), bf16[8,160,1536]{2,0,1:T(8,128)(2,1)}, u32[]{:S(2)}, u32[]{:S(2)}) %all-to-all-start.6) | async-done | bytes 3932192 | tf_op jit(solution)/shard_map/all_to_all | solution.py:246
  298.8 5.1 %all-to-all-start.5 = ((bf16[8,160,1536]{2,0,1:T(8,128)(2,1)}), bf16[8,160,1536]{2,0,1:T(8,128)(2,1)}, u32[]{:S(2)}, u32[]{:S(2)}) async-start(bf16[8,160,1536]{2,0,1:T(8,128)(2,1)} %bitcast.209), calls=%async_computation.5 | async-start | bytes 7864320 | tf_op jit(solution)/shard_map/all_to_all | solution.py:253
  303.9 3.9 fusion.32
  307.8 6.9 %fusion.15 = bf16[32,8,5,1536]{3,1,0,2:T(8,128)(2,1)} fusion(bf16[5,128,1536]{2,1,0:T(8,128)(2,1)S(1)} %copy-done, bf16[5,1536,128]{2,1,0:T(8,128)(2,1)} %param.36, bf16[32,8,5,1536]{3,1,2,0:T(8,128)(2,1)} %bitcast.46, f32[256,5,128]{2,0,1:T(8,128)S(1)} %fusion.32), kind=kOutput, calls=%fused_computation.20 | convolution fusion | flops 1009582080 | bytes 12451840 | tf_op jit(solution)/shard_map/ref,efd->red/dot_general | solution.py:68
  314.7 4.3 %copy.107 = bf16[32,8,5,1536]{3,1,2,0:T(8,128)(2,1)} copy(bf16[32,8,5,1536]{3,1,0,2:T(8,128)(2,1)} %fusion.15) | data formatting | bytes 7864320 | tf_op jit(solution)/shard_map/reshape | solution.py:251
  319.0 32.9 %all-to-all-done.5 = bf16[8,160,1536]{2,0,1:T(8,128)(2,1)} async-done(((bf16[8,160,1536]{2,0,1:T(8,128)(2,1)}), bf16[8,160,1536]{2,0,1:T(8,128)(2,1)}, u32[]{:S(2)}, u32[]{:S(2)}) %all-to-all-start.5) | async-done | bytes 3932192 | tf_op jit(solution)/shard_map/all_to_all | solution.py:253
  351.9 5.7 %all-to-all-start.7 = ((bf16[8,160,1536]{2,0,1:T(8,128)(2,1)}), bf16[8,160,1536]{2,0,1:T(8,128)(2,1)}, u32[]{:S(2)}, u32[]{:S(2)}) async-start(bf16[8,160,1536]{2,0,1:T(8,128)(2,1)} %bitcast.208), calls=%async_computation.7 | async-start | bytes 7864320 | tf_op jit(solution)/shard_map/all_to_all | solution.py:253
  358.8 4.0 reduce_sum.130
  365.6 39.7 %all-to-all-done.7 = bf16[8,160,1536]{2,0,1:T(8,128)(2,1)} async-done(((bf16[8,160,1536]{2,0,1:T(8,128)(2,1)}), bf16[8,160,1536]{2,0,1:T(8,128)(2,1)}, u32[]{:S(2)}, u32[]{:S(2)}) %all-to-all-start.7) | async-done | bytes 3932192 | tf_op jit(solution)/shard_map/all_to_all | solution.py:253
  405.3 4.0 reduce_sum.131
  (162 shorter events, 73.5 us)
Async XLA Ops:
  0.6 254.3 %copy-start = (bf16[5,128,1536]{2,1,0:T(8,128)(2,1)S(1)}, bf16[5,128,1536]{2,1,0:T(8,128)(2,1)}, u32[]{:S(2)}) copy-start(bf16[5,128,1536]{2,1,0:T(8,128)(2,1)} %param.37) | copy-start | bytes 5898244
  15.8 10.5 %copy-start.24 = (s32[8,4]{0,1:T(4,128)S(1)}, s32[8,4]{0,1:T(4,128)}, u32[]{:S(2)}) copy-start(s32[8,4]{0,1:T(4,128)} %param.30) | copy-start | bytes 388
  15.8 10.6 %copy-start.32 = (s32[64]{0:T(128)S(1)}, s32[64]{0:T(128)}, u32[]{:S(2)}) copy-start(s32[64]{0:T(128)} %param.31) | copy-start | bytes 772
  17.5 35.1 %all-to-all-start = ((bf16[8,2,28672]{2,1,0:T(2,128)(2,1)}), bf16[8,2,28672]{2,1,0:T(2,128)(2,1)S(1)}, u32[]{:S(2)}, u32[]{:S(2)}) async-start(bf16[8,2,28672]{2,1,0:T(2,128)(2,1)} %reshape.472), calls=%async_computation | async-start | bytes 1835008 | tf_op jit(solution)/shard_map/all_to_all | solution.py:13
  62.4 5.1 %copy-start.33 = (s32[1,4]{1,0:T(1,128)S(1)}, s32[1,4]{1,0:T(1,128)}, u32[]{:S(2)}) copy-start(s32[1,4]{1,0:T(1,128)} %param.29) | copy-start | bytes 52
  62.4 5.3 %copy-start.22 = (s32[64,8]{0,1:T(8,128)S(1)}, s32[64,8]{0,1:T(8,128)}, u32[]{:S(2)}) copy-start(s32[64,8]{0,1:T(8,128)} %param.33) | copy-start | bytes 6148
  62.4 7.0 %copy-start.4 = (bf16[256,1536]{1,0:T(8,128)(2,1)S(1)}, bf16[256,1536]{1,0:T(8,128)(2,1)}, u32[]{:S(2)}) copy-start(bf16[256,1536]{1,0:T(8,128)(2,1)} %param.19) | copy-start | bytes 2359300
  62.4 7.4 %copy-start.28 = (bf16[1536,128]{1,0:T(8,128)(2,1)S(1)}, bf16[1536,128]{1,0:T(8,128)(2,1)}, u32[]{:S(2)}) copy-start(bf16[1536,128]{1,0:T(8,128)(2,1)} %param.22) | copy-start | bytes 1179652
  62.4 7.4 %copy-start.30 = (f32[1536]{0:T(1024)S(1)}, f32[1536]{0:T(1024)}, u32[]{:S(2)}) copy-start(f32[1536]{0:T(1024)} %param.20) | copy-start | bytes 18436
  62.5 48.3 %all-to-all-start.1 = ((bf16[8,4,57344]{2,1,0:T(4,128)(2,1)}), bf16[8,4,57344]{2,1,0:T(4,128)(2,1)}, u32[]{:S(2)}, u32[]{:S(2)}) async-start(bf16[8,4,57344]{2,1,0:T(4,128)(2,1)} %broadcast_in_dim.172), calls=%async_computation.1 | async-start | bytes 7340032 | tf_op jit(solution)/shard_map/all_to_all | solution.py:129
  67.8 5.3 %copy-start.7 = (s32[64,8]{1,0:T(8,128)}, s32[64,8]{1,0:T(8,128)S(1)}, u32[]{:S(2)}) copy-start(s32[64,8]{1,0:T(8,128)S(1)} %copy.96) | copy-start | bytes 6148
  68.5 4.6 %copy-start.20 = (s32[256]{0:T(256)}, s32[256]{0:T(256)S(1)}, u32[]{:S(2)}) copy-start(s32[256]{0:T(256)S(1)} %iota_add_fusion) | copy-start | bytes 3076
  69.6 48.3 %copy-start.25 = (f32[256]{0:T(256)}, f32[256]{0:T(256)S(1)}, u32[]{:S(2)}) copy-start(f32[256]{0:T(256)S(1)} %add_rsqrt_fusion) | copy-start | bytes 3076
  123.5 3.5 copy-start.29
  123.5 3.5 copy-start.31
  123.5 4.0 copy-start.14
  127.5 5.8 %copy-start.15 = (s32[2048]{0:T(1024)S(1)}, s32[2048]{0:T(1024)}, u32[]{:S(2)}) copy-start(s32[2048]{0:T(1024)} %convert_reduce_fusion) | copy-start | bytes 24580
  127.5 5.8 %copy-start.17 = (s32[256]{0:T(256)S(1)}, s32[256]{0:T(256)}, u32[]{:S(2)}) copy-start(s32[256]{0:T(256)} %copy-done.16) | copy-start | bytes 3076
  127.5 5.8 %copy-start.21 = (s32[256]{0:T(256)S(1)}, s32[256]{0:T(256)}, u32[]{:S(2)}) copy-start(s32[256]{0:T(256)} %copy-done.20) | copy-start | bytes 3076
  128.6 19.6 %all-to-all-start.2 = ((bf16[8,256,256]{1,2,0:T(8,128)(2,1)}), bf16[8,256,256]{1,2,0:T(8,128)(2,1)S(1)}, u32[]{:S(2)}, u32[]{:S(2)}) async-start(bf16[8,256,256]{1,2,0:T(8,128)(2,1)} %broadcast_in_dim.174), calls=%async_computation.2 | async-start | bytes 2097152 | tf_op jit(solution)/shard_map/all_to_all | solution.py:176
  158.2 3.7 copy-start.6
  161.8 5.9 %copy-start.19 = (s32[4,128]{1,0:T(4,128)S(1)}, s32[4,128]{1,0:T(4,128)}, u32[]{:S(2)}) copy-start(s32[4,128]{1,0:T(4,128)} %eq.130) | copy-start | bytes 6148
  161.8 5.9 %copy-start.8 = (s32[64,8]{1,0:T(8,128)S(1)}, s32[64,8]{1,0:T(8,128)}, u32[]{:S(2)}) copy-start(s32[64,8]{1,0:T(8,128)} %copy-done.7) | copy-start | bytes 6148
  163.3 15.7 %copy-start.18 = (f32[1536]{0:T(1024)S(1)}, f32[1536]{0:T(1024)}, u32[]{:S(2)}) copy-start(f32[1536]{0:T(1024)} %param.32) | copy-start | bytes 18436
  163.3 14.4 %all-to-all-start.3 = ((bf16[4,64,1536]{2,1,0:T(8,128)(2,1)}), bf16[4,64,1536]{2,1,0:T(8,128)(2,1)S(1)}, u32[]{:S(2)}, u32[]{:S(2)}) async-start(bf16[4,64,1536]{2,1,0:T(8,128)(2,1)} %bitcast.31), calls=%async_computation.3 | async-start | bytes 1572864 | tf_op jit(solution)/shard_map/all_to_all | solution.py:211
  177.8 4.3 %copy-start.3 = (bf16[64,1536]{1,0:T(8,128)(2,1)}, bf16[64,1536]{1,0:T(8,128)(2,1)S(1)}, u32[]{:S(2)}) copy-start(bf16[64,1536]{1,0:T(8,128)(2,1)S(1)} %reduce_sum.126) | copy-start | bytes 589828
  186.4 55.7 %all-to-all-start.4 = ((bf16[8,160,1536]{2,0,1:T(8,128)(2,1)}), bf16[8,160,1536]{2,0,1:T(8,128)(2,1)}, u32[]{:S(2)}, u32[]{:S(2)}) async-start(bf16[8,160,1536]{2,0,1:T(8,128)(2,1)} %bitcast.211), calls=%async_computation.4 | async-start | bytes 7864320 | tf_op jit(solution)/shard_map/all_to_all | solution.py:246
  245.6 53.2 %all-to-all-start.6 = ((bf16[8,160,1536]{2,0,1:T(8,128)(2,1)}), bf16[8,160,1536]{2,0,1:T(8,128)(2,1)}, u32[]{:S(2)}, u32[]{:S(2)}) async-start(bf16[8,160,1536]{2,0,1:T(8,128)(2,1)} %bitcast.210), calls=%async_computation.6 | async-start | bytes 7864320 | tf_op jit(solution)/shard_map/all_to_all | solution.py:246
  298.8 53.1 %all-to-all-start.5 = ((bf16[8,160,1536]{2,0,1:T(8,128)(2,1)}), bf16[8,160,1536]{2,0,1:T(8,128)(2,1)}, u32[]{:S(2)}, u32[]{:S(2)}) async-start(bf16[8,160,1536]{2,0,1:T(8,128)(2,1)} %bitcast.209), calls=%async_computation.5 | async-start | bytes 7864320 | tf_op jit(solution)/shard_map/all_to_all | solution.py:253
  351.9 5.7 %copy-start.23 = (f32[64,8]{0,1:T(8,128)S(1)}, f32[64,8]{0,1:T(8,128)}, u32[]{:S(2)}) copy-start(f32[64,8]{0,1:T(8,128)} %param.34) | copy-start | bytes 6148
  351.9 5.8 %copy-start.11 = (s32[64,8]{1,0:T(8,128)S(1)}, s32[64,8]{1,0:T(8,128)}, u32[]{:S(2)}) copy-start(s32[64,8]{1,0:T(8,128)} %copy-done.10) | copy-start | bytes 6148
  351.9 53.4 %all-to-all-start.7 = ((bf16[8,160,1536]{2,0,1:T(8,128)(2,1)}), bf16[8,160,1536]{2,0,1:T(8,128)(2,1)}, u32[]{:S(2)}, u32[]{:S(2)}) async-start(bf16[8,160,1536]{2,0,1:T(8,128)(2,1)} %bitcast.208), calls=%async_computation.7 | async-start | bytes 7864320 | tf_op jit(solution)/shard_map/all_to_all | solution.py:253
  (11 other events, 22.9 us)
